TPU v7x, 128 devices: a whole 4x4x4 slice. The times are simulated.
128 devices in a mesh: wave: 8 (over z_lo, x), strip: 16 (over y, z_hi, core).
Axes of the slice: x: 4, y: 4, z: 4 (z_hi: 2, z_lo: 2; z = z_hi * 2 + z_lo), core: 2. Of those that a mesh axis runs over, the one named last changes fastest.
Arguments:
- unit_params: float32 [9, 16, 24576], P(None, 'strip', 'wave'), may hold values from 0 to 1
- observed: bfloat16 [4, 256, 1536, 256], P(None, 'wave', 'strip'), may hold values from -3 to 3
- psf_rows: bfloat16 [256, 4, 65], P('wave'), may hold values from -0.75 to 0.75
- psf_cols: bfloat16 [256, 4, 65], P('wave'), may hold values from -0.75 to 0.75
- pixel_mask: int32 [1536, 256], P('strip'), may hold values 0 or 1
- strip_lengths: int32 [16], P('strip'), may hold values from 32 to 96, as said below
Outputs:
- param_grad: float32 [9, 16, 24576], P(None, 'strip', 'wave')
Inputs may be any that keep to these rules, and one draw needn't show every extreme that they name: `strip_lengths`: the strip lengths sum to 1024; in every draw one strip holds 96 rows and one holds 32.
All inputs are finite; a program needn't handle non-finite values. No bound on the sum of `pixel_mask` on one device may be relied on, other than what follows from the above.
Results may differ from a plain program's by a relative error of at most 0.00098.
Values may be sent and summed in bfloat16 or wider, within the bound.
No kernel may reach another device: no remote copies, remote signals or barrier semaphores. Data moves between devices by JAX's collectives and lax.ppermute only.
A program may use at most 192 MiB of HBM per device.

v0:
```python
import jax
import jax.numpy as jnp
from jax import lax
from jax.sharding import PartitionSpec as P

parameter_low = (0.2, 0.4, 2.0, -0.8, 0.4, 0.3, 0.0, 0.0, 0.0)
parameter_span = (0.4, 0.6, 18.0, 1.6, 0.8, 1.2, 1.5, 3.141592653589793, 3.141592653589793)
stokes_weight = (1.0, 3.0, 3.0, 2.0)
loss_scale = 0.03125


def passed_along(shard, axis, by):
    count = lax.axis_size(axis)
    pairs = [(i, i + by) for i in range(count) if 0 <= i + by < count]
    return lax.ppermute(shard, axis, pairs)


def profile(distance, damping):
    scaled = distance / damping
    return 1.0 / (1.0 + scaled * scaled)


def stokes_model(unit_params, wave_grid):
    physical = [
        parameter_low[number] + parameter_span[number] * unit_params[number] for number in range(9)
    ]
    (
        source_zero,
        source_slope,
        strength,
        doppler,
        line_width,
        damping,
        zeeman_split,
        incline,
        azimuth,
    ) = physical
    offset = (wave_grid[:, None, None] - doppler) / line_width
    split_ratio = zeeman_split / line_width
    centre = profile(offset, damping)
    upper_line = profile(offset - split_ratio, damping)
    lower_line = profile(offset + split_ratio, damping)
    cosine = jnp.cos(incline)
    sine_value = jnp.sin(incline)
    sine_square = sine_value * sine_value
    absorb_total = 1.0 + strength * (
        centre * sine_square * 0.5 + (upper_line + lower_line) * (1.0 + cosine * cosine) * 0.25
    )
    linear = strength * (centre - 0.5 * (upper_line + lower_line)) * sine_square * 0.5
    linear_cosine = linear * jnp.cos(2.0 * azimuth)
    linear_sine = linear * jnp.sin(2.0 * azimuth)
    circular = strength * (lower_line - upper_line) * cosine * 0.5
    denominator = (
        absorb_total * absorb_total
        - linear_cosine * linear_cosine
        - linear_sine * linear_sine
        - circular * circular
    )
    source_ratio = source_slope / denominator
    return jnp.stack(
        [
            source_zero + source_ratio * absorb_total,
            -source_ratio * linear_cosine,
            -source_ratio * linear_sine,
            -source_ratio * circular,
        ]
    )


def band_tables(tap_table, out_rows, tap_count):
    in_rows = out_rows + tap_count - 1
    target_row = lax.broadcasted_iota(jnp.int32, (out_rows, in_rows, tap_count), 0)
    source_row = lax.broadcasted_iota(jnp.int32, (out_rows, in_rows, tap_count), 1)
    tap_index = lax.broadcasted_iota(jnp.int32, (out_rows, in_rows, tap_count), 2)
    selector = (source_row - target_row == tap_index).astype(jnp.bfloat16)
    return jnp.einsum(
        "wkt,ijt->wkij", tap_table, selector, preferred_element_type=jnp.float32
    ).astype(jnp.bfloat16)


def column_tables(tap_table, columns, tap_count):
    radius = tap_count // 2
    source_column = lax.broadcasted_iota(jnp.int32, (columns, columns, tap_count), 0)
    target_column = lax.broadcasted_iota(jnp.int32, (columns, columns, tap_count), 1)
    tap_index = lax.broadcasted_iota(jnp.int32, (columns, columns, tap_count), 2)
    selector = (source_column - target_column + radius == tap_index).astype(jnp.bfloat16)
    return jnp.einsum(
        "wkt,xyt->wkxy", tap_table, selector, preferred_element_type=jnp.float32
    ).astype(jnp.bfloat16)


def extend(upper_rim, middle, lower_rim, length, axis_index):
    radius = upper_rim.shape[axis_index]
    widened = jnp.concatenate([upper_rim, middle, jnp.zeros_like(upper_rim)], axis=axis_index)
    return lax.dynamic_update_slice_in_dim(widened, lower_rim, radius + length, axis_index)


def per_device(unit_params, observed, psf_rows, psf_cols, pixel_mask, strip_lengths):
    stokes_count, wave_count, capacity, columns = observed.shape
    tap_count = psf_rows.shape[2]
    radius = tap_count // 2
    gathered = lax.all_gather(unit_params, "wave", axis=2, tiled=True)
    own_params = gathered.reshape(gathered.shape[0], capacity, columns)
    length = strip_lengths[0]
    wave_pos = lax.axis_index("wave")
    levels = (wave_pos * wave_count + jnp.arange(wave_count, dtype=jnp.int32)).astype(jnp.float32)
    wave_grid = -3.0 + 6.0 * levels / (wave_count * lax.axis_size("wave") - 1)
    row_index = jnp.arange(capacity, dtype=jnp.int32)
    rows_live = (row_index < length).astype(jnp.float32)
    model_own = (stokes_model(own_params, wave_grid) * rows_live[:, None]).astype(jnp.bfloat16)
    tail_rows = lax.dynamic_slice_in_dim(model_own, length - radius, radius, 2)
    upper_rim = passed_along(tail_rows, "strip", 1)
    lower_rim = passed_along(model_own[:, :, :radius], "strip", -1)
    model_wide = extend(upper_rim, model_own, lower_rim, length, 2)
    row_band = band_tables(psf_rows, capacity, tap_count)
    column_band = column_tables(psf_cols, columns, tap_count)
    live_mask = pixel_mask.astype(jnp.float32) * rows_live[:, None]
    weight_square = jnp.array(stokes_weight, jnp.float32)
    weight_square = weight_square * weight_square
    block_size = 4
    block_count = wave_count // block_size

    def forward(number, residual_all):
        first_wave = number * block_size
        model_block = lax.dynamic_slice_in_dim(model_wide, first_wave, block_size, 1)
        band_block = lax.dynamic_slice_in_dim(row_band, first_wave, block_size, 0)
        column_block = lax.dynamic_slice_in_dim(column_band, first_wave, block_size, 0)
        observed_block = lax.dynamic_slice_in_dim(observed, first_wave, block_size, 1)
        row_pass = jnp.einsum(
            "wkij,swjc->kswic", band_block, model_block, preferred_element_type=jnp.float32
        ).astype(jnp.bfloat16)
        blurred = jnp.einsum(
            "kswic,wkcd->swid", row_pass, column_block, preferred_element_type=jnp.float32
        )
        residual = (
            loss_scale
            * weight_square[:, None, None, None]
            * live_mask
            * (blurred - observed_block.astype(jnp.float32))
        ).astype(jnp.bfloat16)
        return lax.dynamic_update_slice_in_dim(residual_all, residual, first_wave, 1)

    residual_all = lax.fori_loop(0, block_count, forward, jnp.zeros(observed.shape, jnp.bfloat16))
    row_back = band_tables(psf_rows[:, :, ::-1], capacity, tap_count)
    tail_residual = lax.dynamic_slice_in_dim(residual_all, length - radius, radius, 2)
    upper_resid = passed_along(tail_residual, "strip", 1)
    lower_resid = passed_along(residual_all[:, :, :radius], "strip", -1)
    residual_wide = extend(upper_resid, residual_all, lower_resid, length, 2)

    def backward(number, gradient_sum):
        first_wave = number * block_size
        residual_block = lax.dynamic_slice_in_dim(residual_wide, first_wave, block_size, 1)
        column_block = lax.dynamic_slice_in_dim(column_band, first_wave, block_size, 0)
        back_block = lax.dynamic_slice_in_dim(row_back, first_wave, block_size, 0)
        grid_block = lax.dynamic_slice_in_dim(wave_grid, first_wave, block_size, 0)
        across = jnp.einsum(
            "swjc,wkdc->kswjd", residual_block, column_block, preferred_element_type=jnp.float32
        ).astype(jnp.bfloat16)
        adjoint = (
            jnp.einsum("wkij,kswjc->swic", back_block, across, preferred_element_type=jnp.float32)
            * rows_live[:, None]
        )

        def model_of(params_now):
            return stokes_model(params_now, grid_block)

        unused_model, pullback = jax.vjp(model_of, own_params)
        return gradient_sum + pullback(adjoint)[0]

    gradient_local = lax.fori_loop(
        0, block_count, backward, jnp.zeros(own_params.shape, jnp.float32)
    )
    gradient_flat = gradient_local.reshape(gathered.shape)
    gradient_total = lax.psum(gradient_flat, "wave")
    share_width = unit_params.shape[2]
    return lax.dynamic_slice_in_dim(gradient_total, wave_pos * share_width, share_width, 2)


def solution(mesh):
    return jax.shard_map(
        per_device,
        mesh=mesh,
        in_specs=(
            P(None, "strip", "wave"),
            P(None, "wave", "strip", None),
            P("wave", None, None),
            P("wave", None, None),
            P("strip", None),
            P("strip"),
        ),
        out_specs=P(None, "strip", "wave"),
        check_vma=False,
    )
```

profile of v0, /device:TPU:0, one launch (start us, length us, event | category | flops | bytes accessed | tf_op | source)
XLA Modules:
  0.0 510.9 jit_solution(6636742498582574275)
XLA Ops:
  6.5 31.1 %all_gather.3 = f32[9,1,24576]{2,1,0:T(1,128)S(1)} all-gather(f32[9,1,3072]{2,1,0:T(1,128)} %param.11), channel_id=1, replica_groups=mesh['wave'=8,'strip'=16] {'wave'}, dimensions={2}, use_global_device_ids=true | all-gather | bytes 995328 | tf_op jit(solution)/shard_map/all_gather | solution.py:102
  37.6 9.9 %fusion.103 = (f32[24576]{0:T(1024)S(1)}, f32[24576]{0:T(1024)S(1)}, f32[24576]{0:T(1024)S(1)}, f32[24576]{0:T(1024)S(1)}, f32[24576]{0:T(1024)S(1)}, /*index=5*...) fusion(f32[9,1,24576]{2,1,0:T(1,128)S(1)} %all_gather.3), kind=kLoop, calls=%fused_computation.198 | loop fusion | flops 442368 | bytes 1966080 | tf_op jit(solution)/shard_map/add | solution.py:25
  48.7 5.3 %multiply_add_fusion.8 = (f32[1,32,96,256]{3,2,1,0:T(8,128)S(1)}, f32[1,32,96,256]{3,2,1,0:T(8,128)S(1)}, f32[1,32,96,256]{3,2,1,0:T(8,128)S(1)}, f32[1,32,96,256]{3,2,1,0:T(8,128)S(1)}) fusion(f32[96,256]{1,0:T(8,128)S(1)} %get-tuple-element.546, f32[96,256]{1,0:T(8,128)S(1)} %add.585, f32[96,256]{1,0:T(8,128)S(1)} %get-tuple-element.545, ...), kind=kLoop, calls=%fused_computation.166 | loop fusion | flops 37748736 | bytes 13860992 | tf_op jit(solution)/shard_map/add | solution.py:62
  54.0 2.0 fusion.74
  56.1 3.7 fusion.113
  60.0 2.6 collective-permute-start
  64.1 8.5 %convert_bitcast_fusion = bf16[32,4,256,256]{3,0,1,2:T(8,128)(2,1)} fusion(bf16[32,4,65]{2,1,0:T(4,128)(2,1)S(1)} %copy-done.4), kind=kOutput, calls=%fused_computation.149 | convolution fusion | flops 1111687168 | bytes 16793856 | tf_op jit(solution)/shard_map/wkt,xyt->wkxy/dot_general | solution.py:87
  72.6 16.3 %copy.20 = bf16[32,4,256,256]{3,2,1,0:T(8,128)(2,1)} copy(bf16[32,4,256,256]{3,0,1,2:T(8,128)(2,1)} %convert_bitcast_fusion) | data formatting | bytes 33554432
  89.0 3.9 convert_bitcast_fusion.2
  92.9 10.1 %maximum_maximum_fusion = bf16[4,32,160,256]{3,2,1,0:T(8,128)(2,1)} fusion(bf16[4,32,96,256]{3,2,1,0:T(8,128)(2,1)} %copy-done.1, bf16[4,32,32,256]{3,2,1,0:T(8,128)(2,1)} %collective-permute-done, bf16[160]{0:T(256)(128)(2,1)S(1)} %pad.113.clone), kind=kLoop, calls=%fused_computation.152 | loop fusion | flops 31457280 | bytes 18874688 | tf_op jit(solution)/shard_map/concatenate | solution.py:94
  103.0 20.4 %dynamic_update_slice.13 = bf16[4,32,160,256]{3,2,1,0:T(8,128)(2,1)} dynamic-update-slice(bf16[4,32,160,256]{3,2,1,0:T(8,128)(2,1)} %maximum_maximum_fusion, bf16[4,32,32,256]{3,2,1,0:T(8,128)(2,1)} %collective-permute-done.1, s32[]{:T(128)} %constant.278.clone.1, s32[]{:T(128)} %constant.278.clone.1, s32[]{:T(128)S(6)} %select_n.37, s32[]{:T(128)} %constant.278.clone.1) | dynamic-update-slice | bytes 4194308 | tf_op jit(solution)/shard_map/dynamic_update_slice | solution.py:95
  123.3 3.4 broadcast_in_dim.105.clone
  126.7 58.5 %while.31 = (s32[]{:T(128)}, bf16[4,32,96,256]{3,2,1,0:T(8,128)(2,1)}, f32[96,256]{1,0:T(8,128)S(1)}, bf16[32,4,256,256]{3,2,1,0:T(8,128)(2,1)}, bf16[4,32,160,2...) while((s32[]{:T(128)}, ...), condition=%wide.region_1.0_spmd.clone, body=%wide.region_0.0_spmd.clone.sunk | while | flops 1311866880 | bytes 9897691 | solution.py:143
  126.7 1.7 constant_dynamic-slice_fusion.11
  129.1 4.0 fusion.130
  134.0 1.7 constant_dynamic-slice_fusion.11
  136.4 4.0 fusion.130
  141.3 1.7 constant_dynamic-slice_fusion.11
  143.7 4.0 fusion.130
  148.6 1.7 constant_dynamic-slice_fusion.11
  151.0 4.0 fusion.130
  155.9 1.7 constant_dynamic-slice_fusion.11
  158.3 4.0 fusion.130
  163.2 1.7 constant_dynamic-slice_fusion.11
  165.6 4.0 fusion.130
  170.6 1.7 constant_dynamic-slice_fusion.11
  173.0 4.0 fusion.130
  177.9 1.7 constant_dynamic-slice_fusion.11
  180.3 4.0 fusion.130
  185.2 5.4 %fusion.112 = (bf16[4,32,32,256]{3,2,1,0:T(8,128)(2,1)}, bf16[4,32,32,256]{3,2,1,0:T(8,128)(2,1)}) fusion(bf16[4,32,96,256]{3,2,1,0:T(8,128)(2,1)} %get-tuple-element.364, s32[]{:T(128)S(6)} %select_n.36), kind=kLoop, calls=%fused_computation.217 | loop fusion | bytes 8388612 | tf_op jit(solution)/shard_map/slice | solution.py:147
  190.6 22.0 %collective-permute-start.2 = (bf16[4,32,32,256]{3,2,1,0:T(8,128)(2,1)}, bf16[4,32,32,256]{3,2,1,0:T(8,128)(2,1)}, u32[]{:S(2)}, u32[]{:S(2)}) collective-permute-start(bf16[4,32,32,256]{3,2,1,0:T(8,128)(2,1)} %get-tuple-element.537), channel_id=1, source_target_pairs={{0,1},{1,2},{2,3},{3,4},{4,5},{5,6},{6,7},{7,8},{8,9},{9,10},{10,1... | collective-permute-start | bytes 6291464 | tf_op jit(solution)/shard_map/ppermute | solution.py:15
  212.6 1.5 collective-permute-start.3
  214.2 3.6 reduce.1
  217.8 1.9 copy.40
  219.7 4.0 convert_bitcast_fusion.1
  223.7 7.9 %maximum_maximum_fusion.1 = bf16[4,32,160,256]{3,2,1,0:T(8,128)(2,1)} fusion(bf16[4,32,96,256]{3,2,1,0:T(8,128)(2,1)S(1)} %copy-done, bf16[4,32,32,256]{3,2,1,0:T(8,128)(2,1)} %collective-permute-done.2, bf16[160]{0:T(256)(128)(2,1)S(1)} %pad.113.clone), kind=kLoop, calls=%fused_computation.153 | loop fusion | flops 31457280 | bytes 18874688 | tf_op jit(solution)/shard_map/concatenate | solution.py:94
  231.6 20.4 %dynamic_update_slice.14 = bf16[4,32,160,256]{3,2,1,0:T(8,128)(2,1)} dynamic-update-slice(bf16[4,32,160,256]{3,2,1,0:T(8,128)(2,1)} %maximum_maximum_fusion.1, bf16[4,32,32,256]{3,2,1,0:T(8,128)(2,1)} %collective-permute-done.3, s32[]{:T(128)} %constant.278.clone.1, s32[]{:T(128)} %constant.278.clone.1, s32[]{:T(128)S(6)} %select_n.37, s32[]{:T(128)} %constant.278.clone.1) | dynamic-update-slice | bytes 4194308 | tf_op jit(solution)/shard_map/dynamic_update_slice | solution.py:95
  252.0 134.8 %while.32 = (s32[]{:T(128)}, f32[9,96,256]{2,1,0:T(8,128)S(1)}, f32[9,96,256]{2,1,0:T(8,128)S(1)}, f32[32]{0:T(128)S(1)}, bf16[32,4,256,256]{3,2,1,0:T(8,128)(2,...) while((s32[]{:T(128)}, f32[9,96,256]{2,1,0:T(8,128)S(1)}, ...), condition=%wide.region_21.22_spmd.clone, body=%wide.region_2.21_spmd.clone.sunk | while | flops 1872642304 | bytes 34342920 | solution.py:170
  252.0 2.5 constant_dynamic-slice_fusion.12
  255.2 4.9 fusion.134
  265.2 1.5 fusion.136
  268.8 2.5 constant_dynamic-slice_fusion.12
  272.0 4.9 fusion.134
  282.0 1.5 fusion.136
  285.7 2.5 constant_dynamic-slice_fusion.12
  288.9 4.9 fusion.134
  298.9 1.5 fusion.136
  302.5 2.5 constant_dynamic-slice_fusion.12
  305.7 4.9 fusion.134
  315.7 1.5 fusion.136
  319.4 2.5 constant_dynamic-slice_fusion.12
  322.6 4.9 fusion.134
  332.6 1.5 fusion.136
  336.2 2.5 constant_dynamic-slice_fusion.12
  339.4 4.9 fusion.134
  349.5 1.5 fusion.136
  353.1 2.5 constant_dynamic-slice_fusion.12
  356.3 4.9 fusion.134
  366.3 1.5 fusion.136
  369.9 2.5 constant_dynamic-slice_fusion.12
  373.1 4.9 fusion.134
  386.8 1.8 reshape.646
  388.6 113.9 %all-reduce.11.cloned.1.call-done = f32[9,1,24576]{2,1,0:T(1,128)} async-done(((f32[9,1,24576]{2,1,0:T(1,128)}), f32[9,1,24576]{2,1,0:T(1,128)}) %all-reduce.11.cloned.1.call-update) | async-done | bytes 884752 | tf_op jit(solution)/shard_map/psum | solution.py:174
  502.5 1.5 constant_dynamic-slice_fusion.3
  (176 shorter events, 80.4 us)
Async XLA Ops:
  6.5 496.0 %all-reduce.11.cloned.1.call-start = ((), (), s32[]{:S(2)}) async-start(), calls=%async_computation | async-start | bytes 1769472 | tf_op jit(solution)/shard_map/psum | solution.py:174
  56.1 3.9 copy-start.1
  56.1 8.0 %copy-start.4 = (bf16[32,4,65]{2,1,0:T(4,128)(2,1)S(1)}, bf16[32,4,65]{2,1,0:T(4,128)(2,1)}, u32[]{:S(2)}) copy-start(bf16[32,4,65]{2,1,0:T(4,128)(2,1)} %param.14) | copy-start | bytes 49924
  60.0 32.9 %collective-permute-start = (bf16[4,32,32,256]{3,2,1,0:T(8,128)(2,1)}, bf16[4,32,32,256]{3,2,1,0:T(8,128)(2,1)}, u32[]{:S(2)}, u32[]{:S(2)}) collective-permute-start(bf16[4,32,32,256]{3,2,1,0:T(8,128)(2,1)} %get-tuple-element.539), channel_id=1, source_target_pairs={{0,1},{1,2},{2,3},{3,4},{4,5},{5,6},{6,7},{7,8},{8,9},{9,10},{10,1... | collective-permute-start | bytes 6291464 | tf_op jit(solution)/shard_map/ppermute | solution.py:15
  62.6 40.3 %collective-permute-start.1 = (bf16[4,32,32,256]{3,2,1,0:T(8,128)(2,1)}, bf16[4,32,32,256]{3,2,1,0:T(8,128)(2,1)}, u32[]{:S(2)}, u32[]{:S(2)}) collective-permute-start(bf16[4,32,32,256]{3,2,1,0:T(8,128)(2,1)} %get-tuple-element.538), channel_id=1, source_target_pairs={{1,0},{2,1},{3,2},{4,3},{5,4},{6,5},{7,6},{8,7},{9,8},{10,9},{11,1... | collective-permute-start | bytes 6291464 | tf_op jit(solution)/shard_map/ppermute | solution.py:15
  72.6 16.4 %copy-start.3 = (s32[96,256]{1,0:T(8,128)S(1)}, s32[96,256]{1,0:T(8,128)}, u32[]{:S(2)}) copy-start(s32[96,256]{1,0:T(8,128)} %param.15) | copy-start | bytes 294916
  72.6 16.4 %copy-start.2 = (bf16[32,4,65]{2,1,0:T(4,128)(2,1)S(1)}, bf16[32,4,65]{2,1,0:T(4,128)(2,1)}, u32[]{:S(2)}) copy-start(bf16[32,4,65]{2,1,0:T(4,128)(2,1)} %param.13) | copy-start | bytes 49924
  123.3 3.4 copy-start.5
  190.6 33.1 %collective-permute-start.2 = (bf16[4,32,32,256]{3,2,1,0:T(8,128)(2,1)}, bf16[4,32,32,256]{3,2,1,0:T(8,128)(2,1)}, u32[]{:S(2)}, u32[]{:S(2)}) collective-permute-start(bf16[4,32,32,256]{3,2,1,0:T(8,128)(2,1)} %get-tuple-element.537), channel_id=1, source_target_pairs={{0,1},{1,2},{2,3},{3,4},{4,5},{5,6},{6,7},{7,8},{8,9},{9,10},{10,1... | collective-permute-start | bytes 6291464 | tf_op jit(solution)/shard_map/ppermute | solution.py:15
  212.6 19.0 %collective-permute-start.3 = (bf16[4,32,32,256]{3,2,1,0:T(8,128)(2,1)}, bf16[4,32,32,256]{3,2,1,0:T(8,128)(2,1)}, u32[]{:S(2)}, u32[]{:S(2)}) collective-permute-start(bf16[4,32,32,256]{3,2,1,0:T(8,128)(2,1)} %get-tuple-element.536), channel_id=1, source_target_pairs={{1,0},{2,1},{3,2},{4,3},{5,4},{6,5},{7,6},{8,7},{9,8},{10,9},{11,1... | collective-permute-start | bytes 6291464 | tf_op jit(solution)/shard_map/ppermute | solution.py:15
  219.7 4.0 copy-start
Sparse Core Ops, SparseCore 0:
  388.8 113.6 all-reduce.10
where the time goes:
time: 514 us; the launch traced here: 511 us
  local copies, waits for them, and re-layouts  122 us (24%)
  other arithmetic  114 us (22%)
  waiting for transfers between devices  114 us (22%)
  matrix products  87 us (17%)
  blocking collectives  31.1 us (6%)
  starting transfers between devices  27.5 us (5%)
  between operations  14.3 us (3%)
    psum x1, waiting for transfers between devices, per_device(): gradient_total = lax.psum(gradient_flat, 'wave')  114 us
    dynamic_update_slice x2, local copies, waits for them, and re-layouts, extend(): lax.dynamic_update_slice_in_dim(widened, lower_rim, radius + length, axis...  40.8 us
    dot_general x8, matrix products, backward(): jnp.einsum('wkij,kswjc->swic', back_block, across, preferred_element_type...  39.1 us
    dot_general x8, matrix products, forward(): jnp.einsum('kswic,wkcd->swid', row_pass, column_block, preferred_element_...  31.6 us
    all_gather x1, blocking collectives, per_device(): gathered = lax.all_gather(unit_params, 'wave', axis=2, tiled=True)  31.1 us
    ppermute x4, starting transfers between devices, passed_along(): return lax.ppermute(shard, axis, pairs)  27.5 us
    mul x32, other arithmetic, stokes_model(): parameter_span[number] * unit_params[number]  22.7 us
    dynamic_slice x8, local copies, waits for them, and re-layouts, backward(): back_block = lax.dynamic_slice_in_dim(row_back, first_wave, block_size, 0)  20.2 us
  transfers between devices with their start and end apart: 5, of which 1 were waited for; matrix products, arithmetic and copies ran while one was open for 11% of the time, Pallas kernels for 0%

commit v1 on v0

--- a/solution.py
+++ b/solution.py
@@ -1,3 +1,4 @@
+import functools
 import jax
 import jax.numpy as jnp
 from jax import lax
@@ -7,6 +8,19 @@
 parameter_span = (0.4, 0.6, 18.0, 1.6, 0.8, 1.2, 1.5, 3.141592653589793, 3.141592653589793)
 stokes_weight = (1.0, 3.0, 3.0, 2.0)
 loss_scale = 0.03125
+
+
+def _create_loads(x_part, on_dim):
+    history = []
+    for _ in range(lax.axis_size("wave")):
+        history.append(x_part)
+    front = jnp.stack(history)
+    lower = lax.all_to_all(front, axis_name="wave", split_axis=0, concat_axis=0)
+    part_now = jnp.concatenate(lower, axis=on_dim)
+    return part_now
+
+
+entries_check = functools.partial(_create_loads, on_dim=2)
 
 
 def passed_along(shard, axis, by):
@@ -99,7 +113,7 @@
     stokes_count, wave_count, capacity, columns = observed.shape
     tap_count = psf_rows.shape[2]
     radius = tap_count // 2
-    gathered = lax.all_gather(unit_params, "wave", axis=2, tiled=True)
+    gathered = entries_check(unit_params)
     own_params = gathered.reshape(gathered.shape[0], capacity, columns)
     length = strip_lengths[0]
     wave_pos = lax.axis_index("wave")

time: 514 us -> 499 us (0.971)
  blocking collectives: 31.1 us -> 0 us
  waiting for transfers between devices: 114 us -> 131 us
  local copies, waits for them, and re-layouts: 122 us -> 110 us
  matrix products: 87 us -> 94.7 us
  starting transfers between devices: 27.5 us -> 33.1 us
    all_gather x1 -> x0, blocking collectives: 31.1 us -> none  [per_device(): gathered = lax.all_gather(unit_params, 'wave', axis=2, tiled=True)]
    all_to_all x0 -> x1, waiting for transfers between devices: none -> 13.2 us  [_create_loads(): lower = lax.all_to_all(front, axis_name='wave', split_axis=0, concat_axis=0)]
    dot_general x8, matrix products: 31.6 us -> 39.4 us  [forward(): jnp.einsum('kswic,wkcd->swid', row_pass, column_block, preferred_element_...]
    dynamic_update_slice x8 -> x0, local copies, waits for them, and re-layouts: 7.64 us -> none  [forward(): lax.dynamic_update_slice_in_dim(residual_all, residual, first_wave, 1)]
    all_to_all x0 -> x1, starting transfers between devices: none -> 5.77 us  [_create_loads(): lower = lax.all_to_all(front, axis_name='wave', split_axis=0, concat_axis=0)]
    dynamic_slice x16 -> x8, local copies, waits for them, and re-layouts: 18.2 us -> 13.3 us  [forward(): band_block = lax.dynamic_slice_in_dim(row_band, first_wave, block_size, 0)]
    unnamed x14 -> x12, local copies, waits for them, and re-layouts: 18.4 us -> 17.5 us
  transfers between devices with their start and end apart: 5 -> 6, of which waited for: 1 -> 2; matrix products, arithmetic and copies ran while one was open for 11% -> 11% of each run, Pallas kernels for 0% -> 0%
where the time goes in v1:
time: 499 us; the launch traced here: 495 us
  waiting for transfers between devices  131 us (26%)
  other arithmetic  112 us (22%)
  local copies, waits for them, and re-layouts  110 us (22%)
  matrix products  94.7 us (19%)
  starting transfers between devices  33.1 us (7%)
  between operations  14.3 us (3%)
    psum x1, waiting for transfers between devices, per_device(): gradient_total = lax.psum(gradient_flat, 'wave')  117 us
    dynamic_update_slice x2, local copies, waits for them, and re-layouts, extend(): lax.dynamic_update_slice_in_dim(widened, lower_rim, radius + length, axis...  40.4 us
    dot_general x8, matrix products, forward(): jnp.einsum('kswic,wkcd->swid', row_pass, column_block, preferred_element_...  39.4 us
    dot_general x8, matrix products, backward(): jnp.einsum('wkij,kswjc->swic', back_block, across, preferred_element_type...  39 us
    ppermute x4, starting transfers between devices, passed_along(): return lax.ppermute(shard, axis, pairs)  27.3 us
    mul x32, other arithmetic, stokes_model(): parameter_span[number] * unit_params[number]  22.7 us
    concatenate x2, other arithmetic, extend(): jnp.concatenate([upper_rim, middle, jnp.zeros_like(upper_rim)], axis=axis...  20.4 us
    dynamic_slice x8, local copies, waits for them, and re-layouts, backward(): back_block = lax.dynamic_slice_in_dim(row_back, first_wave, block_size, 0)  20.2 us
  transfers between devices with their start and end apart: 6, of which 2 were waited for; matrix products, arithmetic and copies ran while one was open for 11% of the time, Pallas kernels for 0%

profile of v1, /device:TPU:0, one launch (start us, length us, event | category | flops | bytes accessed | tf_op | source)
XLA Modules:
  0.0 495.4 jit_solution(8865947715357919205)
XLA Ops:
  8.8 5.8 %all-to-all-start = ((f32[8,9,1,3072]{3,2,1,0:T(1,128)}), f32[8,9,1,3072]{3,2,1,0:T(1,128)S(1)}, u32[]{:S(2)}, u32[]{:S(2)}) async-start(f32[8,9,1,3072]{3,2,1,0:T(1,128)} %stack.4), calls=%async_computation | async-start | bytes 1769472 | tf_op jit(solution)/shard_map/all_to_all | solution.py:18
  15.3 13.2 %all-to-all-done = f32[8,9,1,3072]{3,2,1,0:T(1,128)S(1)} async-done(((f32[8,9,1,3072]{3,2,1,0:T(1,128)}), f32[8,9,1,3072]{3,2,1,0:T(1,128)S(1)}, u32[]{:S(2)}, u32[]{:S(2)}) %all-to-all-start) | async-done | bytes 884768 | tf_op jit(solution)/shard_map/all_to_all | solution.py:18
  28.6 8.7 %fusion.111 = (f32[8,3072]{1,0:T(8,128)S(1)}, f32[8,3072]{1,0:T(8,128)S(1)}, f32[8,3072]{1,0:T(8,128)S(1)}, f32[8,3072]{1,0:T(8,128)S(1)}, f32[8,3072]{1,0:T(8,1...) fusion(f32[9,1,8,3072]{3,1,0,2:T(1,128)S(1)} %bitcast.276), kind=kLoop, calls=%fused_computation.199 | loop fusion | flops 442368 | bytes 1966080 | tf_op jit(solution)/shard_map/add | solution.py:39
  37.7 5.3 %multiply_add_fusion.8 = (f32[1,32,96,256]{3,2,0,1:T(8,128)S(1)}, f32[1,32,96,256]{3,2,0,1:T(8,128)S(1)}, f32[1,32,96,256]{3,2,0,1:T(8,128)S(1)}, f32[1,32,96,256]{3,2,0,1:T(8,128)S(1)}) fusion(f32[96,256]{1,0:T(8,128)S(1)} %get-tuple-element.591, f32[96,256]{1,0:T(8,128)S(1)} %add.585, f32[96,256]{1,0:T(8,128)S(1)} %get-tuple-element.590, ...), kind=kLoop, calls=%fused_computation.166 | loop fusion | flops 37748736 | bytes 13860992 | tf_op jit(solution)/shard_map/add | solution.py:76
  43.0 2.1 fusion.82
  45.2 3.7 fusion.121
  49.1 2.9 collective-permute-start
  52.0 1.5 collective-permute-start.1
  53.5 8.5 %convert_bitcast_fusion = bf16[32,4,256,256]{3,0,1,2:T(8,128)(2,1)} fusion(bf16[32,4,65]{2,1,0:T(4,128)(2,1)S(1)} %copy-done.3), kind=kOutput, calls=%fused_computation.149 | convolution fusion | flops 1111687168 | bytes 16793856 | tf_op jit(solution)/shard_map/wkt,xyt->wkxy/dot_general | solution.py:101
  62.0 16.3 %copy.58 = bf16[32,4,256,256]{3,2,1,0:T(8,128)(2,1)} copy(bf16[32,4,256,256]{3,0,1,2:T(8,128)(2,1)} %convert_bitcast_fusion) | data formatting | bytes 33554432
  78.4 3.9 convert_bitcast_fusion.2
  82.3 10.1 %maximum_maximum_fusion = bf16[4,32,160,256]{3,2,0,1:T(8,128)(2,1)} fusion(bf16[4,32,96,256]{3,2,0,1:T(8,128)(2,1)} %copy-done, bf16[4,32,32,256]{3,2,0,1:T(8,128)(2,1)} %collective-permute-done, bf16[160]{0:T(256)(128)(2,1)S(1)} %pad.113.clone), kind=kLoop, calls=%fused_computation.152 | loop fusion | flops 31457280 | bytes 18874688 | tf_op jit(solution)/shard_map/concatenate | solution.py:108
  92.4 20.2 %dynamic_update_slice.13 = bf16[4,32,160,256]{3,2,0,1:T(8,128)(2,1)} dynamic-update-slice(bf16[4,32,160,256]{3,2,0,1:T(8,128)(2,1)} %maximum_maximum_fusion, bf16[4,32,32,256]{3,2,0,1:T(8,128)(2,1)} %collective-permute-done.1, s32[]{:T(128)} %constant.278.clone.1, s32[]{:T(128)} %constant.278.clone.1, s32[]{:T(128)S(6)} %select_n.37, s32[]{:T(128)} %constant.278.clone.1) | dynamic-update-slice | bytes 4194308 | tf_op jit(solution)/shard_map/dynamic_update_slice | solution.py:109
  112.6 3.4 broadcast_in_dim.105
  116.0 53.5 %while.31 = (s32[]{:T(128)}, bf16[4,32,96,256]{3,2,0,1:T(8,128)(2,1)}, f32[96,256]{1,0:T(8,128)S(1)}, bf16[32,4,256,256]{3,2,1,0:T(8,128)(2,1)}, bf16[4,32,160,2...) while((s32[]{:T(128)}, ...), condition=%wide.region_1.0_spmd.clone, body=%wide.region_0.0_spmd.clone.sunk | while | flops 1311866880 | bytes 7342295 | solution.py:157
  116.0 1.7 constant_dynamic-slice_fusion.11
  117.7 4.9 fusion.136
  122.6 1.7 constant_dynamic-slice_fusion.11
  124.4 4.9 fusion.136
  129.3 1.7 constant_dynamic-slice_fusion.11
  131.1 4.9 fusion.136
  136.0 1.7 constant_dynamic-slice_fusion.11
  137.7 5.0 %fusion.136 = bf16[4,32,96,256]{3,2,0,1:T(8,128)(2,1)} fusion(bf16[4,32,96,256]{3,2,0,1:T(8,128)(2,1)} %get-tuple-element.809, s32[]{:T(128)S(6)} %select_n.43, bf16[32,4,256,256]{3,2,1,0:T(8,128)(2,1)} %get-tuple-element.823, bf16[4,32,160,256]{3,2,0,1:T(8,128)(2,1)} %get-tuple-element.824, f32[4,96,256]{2,1,0:T(8,128)S(1)} %broadcast_multiply_fusion.11, ...), kind=kOutput, calls=%fused_computation.11.clone.1 | convolution fusion | flops 1311768576 | bytes 5867520 | tf_op jit(solution)/shard_map/while/body/eval_jaxpr/kswic,wkcd->swid/dot_general | solution.py:146
  142.7 1.7 constant_dynamic-slice_fusion.11
  144.5 4.9 fusion.136
  149.4 1.7 constant_dynamic-slice_fusion.11
  151.2 4.9 fusion.136
  156.1 1.7 constant_dynamic-slice_fusion.11
  157.9 4.9 fusion.136
  162.8 1.7 constant_dynamic-slice_fusion.11
  164.6 4.9 fusion.136
  169.5 5.5 %fusion.120 = (bf16[4,32,32,256]{3,2,0,1:T(8,128)(2,1)}, bf16[4,32,32,256]{3,2,0,1:T(8,128)(2,1)}) fusion(bf16[4,32,96,256]{3,2,0,1:T(8,128)(2,1)} %get-tuple-element.364, s32[]{:T(128)S(6)} %select_n.36), kind=kLoop, calls=%fused_computation.218 | loop fusion | bytes 8388612 | tf_op jit(solution)/shard_map/slice | solution.py:161
  175.0 21.7 %collective-permute-start.2 = (bf16[4,32,32,256]{3,2,0,1:T(8,128)(2,1)}, bf16[4,32,32,256]{3,2,0,1:T(8,128)(2,1)}, u32[]{:S(2)}, u32[]{:S(2)}) collective-permute-start(bf16[4,32,32,256]{3,2,0,1:T(8,128)(2,1)} %get-tuple-element.582), channel_id=1, source_target_pairs={{0,1},{1,2},{2,3},{3,4},{4,5},{5,6},{6,7},{7,8},{8,9},{9,10},{10,1... | collective-permute-start | bytes 6291464 | tf_op jit(solution)/shard_map/ppermute | solution.py:29
  198.1 4.0 convert_bitcast_fusion.1
  202.4 10.3 %maximum_maximum_fusion.1 = bf16[4,32,160,256]{3,2,0,1:T(8,128)(2,1)} fusion(bf16[4,32,96,256]{3,2,0,1:T(8,128)(2,1)} %get-tuple-element.364, bf16[4,32,32,256]{3,2,0,1:T(8,128)(2,1)} %collective-permute-done.2, bf16[160]{0:T(256)(128)(2,1)S(1)} %pad.113.clone), kind=kLoop, calls=%fused_computation.153 | loop fusion | flops 31457280 | bytes 18874688 | tf_op jit(solution)/shard_map/concatenate | solution.py:108
  212.8 20.2 %dynamic_update_slice.14 = bf16[4,32,160,256]{3,2,0,1:T(8,128)(2,1)} dynamic-update-slice(bf16[4,32,160,256]{3,2,0,1:T(8,128)(2,1)} %maximum_maximum_fusion.1, bf16[4,32,32,256]{3,2,0,1:T(8,128)(2,1)} %collective-permute-done.3, s32[]{:T(128)} %constant.278.clone.1, s32[]{:T(128)} %constant.278.clone.1, s32[]{:T(128)S(6)} %select_n.37, s32[]{:T(128)} %constant.278.clone.1) | dynamic-update-slice | bytes 4194308 | tf_op jit(solution)/shard_map/dynamic_update_slice | solution.py:109
  233.0 134.8 %while.32 = (s32[]{:T(128)}, f32[9,96,256]{2,1,0:T(8,128)S(1)}, f32[9,96,256]{2,1,0:T(8,128)S(1)}, f32[32]{0:T(128)S(1)}, bf16[32,4,256,256]{3,2,1,0:T(8,128)(2,...) while((s32[]{:T(128)}, f32[9,96,256]{2,1,0:T(8,128)S(1)}, ...), condition=%wide.region_21.22_spmd.clone, body=%wide.region_2.21_spmd.clone.sunk | while | flops 1872642304 | bytes 34342920 | solution.py:184
  233.0 2.5 constant_dynamic-slice_fusion.12
  236.2 4.9 fusion.140
  246.2 1.5 fusion.142
  249.8 2.5 constant_dynamic-slice_fusion.12
  253.0 4.9 fusion.140
  263.0 1.5 fusion.142
  266.7 2.5 constant_dynamic-slice_fusion.12
  269.9 4.9 fusion.140
  279.9 1.5 fusion.142
  283.5 2.5 constant_dynamic-slice_fusion.12
  286.7 4.9 fusion.140
  296.7 1.5 fusion.142
  300.4 2.5 constant_dynamic-slice_fusion.12
  303.6 4.9 fusion.140
  313.6 1.5 fusion.142
  317.2 2.5 constant_dynamic-slice_fusion.12
  320.4 4.9 fusion.140
  330.4 1.5 fusion.142
  334.1 2.5 constant_dynamic-slice_fusion.12
  337.3 4.9 fusion.140
  347.3 1.5 fusion.142
  350.9 2.5 constant_dynamic-slice_fusion.12
  354.1 4.9 fusion.140
  364.1 1.5 fusion.142
  367.8 1.8 reshape.649
  369.6 117.4 %all-reduce.11.cloned.1.call-done = f32[9,1,24576]{2,1,0:T(1,128)} async-done(((f32[9,1,24576]{2,1,0:T(1,128)}), f32[9,1,24576]{2,1,0:T(1,128)}) %all-reduce.11.cloned.1.call-update) | async-done | bytes 884752 | tf_op jit(solution)/shard_map/psum | solution.py:188
  487.0 1.5 constant_dynamic-slice_fusion.3
  (160 shorter events, 68.8 us)
Async XLA Ops:
  8.8 19.7 %all-to-all-start = ((f32[8,9,1,3072]{3,2,1,0:T(1,128)}), f32[8,9,1,3072]{3,2,1,0:T(1,128)S(1)}, u32[]{:S(2)}, u32[]{:S(2)}) async-start(f32[8,9,1,3072]{3,2,1,0:T(1,128)} %stack.4), calls=%async_computation | async-start | bytes 1769472 | tf_op jit(solution)/shard_map/all_to_all | solution.py:18
  14.6 472.4 %all-reduce.11.cloned.1.call-start = ((), (), s32[]{:S(2)}) async-start(), calls=%async_computation.1 | async-start | bytes 1769472 | tf_op jit(solution)/shard_map/psum | solution.py:188
  45.1 3.9 copy-start
  45.2 8.3 %copy-start.3 = (bf16[32,4,65]{2,1,0:T(4,128)(2,1)S(1)}, bf16[32,4,65]{2,1,0:T(4,128)(2,1)}, u32[]{:S(2)}) copy-start(bf16[32,4,65]{2,1,0:T(4,128)(2,1)} %param.14) | copy-start | bytes 49924
  49.1 33.2 %collective-permute-start = (bf16[4,32,32,256]{3,2,0,1:T(8,128)(2,1)}, bf16[4,32,32,256]{3,2,0,1:T(8,128)(2,1)}, u32[]{:S(2)}, u32[]{:S(2)}) collective-permute-start(bf16[4,32,32,256]{3,2,0,1:T(8,128)(2,1)} %get-tuple-element.584), channel_id=1, source_target_pairs={{0,1},{1,2},{2,3},{3,4},{4,5},{5,6},{6,7},{7,8},{8,9},{9,10},{10,1... | collective-permute-start | bytes 6291464 | tf_op jit(solution)/shard_map/ppermute | solution.py:29
  52.0 40.4 %collective-permute-start.1 = (bf16[4,32,32,256]{3,2,0,1:T(8,128)(2,1)}, bf16[4,32,32,256]{3,2,0,1:T(8,128)(2,1)}, u32[]{:S(2)}, u32[]{:S(2)}) collective-permute-start(bf16[4,32,32,256]{3,2,0,1:T(8,128)(2,1)} %get-tuple-element.583), channel_id=1, source_target_pairs={{1,0},{2,1},{3,2},{4,3},{5,4},{6,5},{7,6},{8,7},{9,8},{10,9},{11,1... | collective-permute-start | bytes 6291464 | tf_op jit(solution)/shard_map/ppermute | solution.py:29
  62.0 16.4 %copy-start.2 = (s32[96,256]{1,0:T(8,128)S(1)}, s32[96,256]{1,0:T(8,128)}, u32[]{:S(2)}) copy-start(s32[96,256]{1,0:T(8,128)} %param.15) | copy-start | bytes 294916
  62.0 16.4 %copy-start.1 = (bf16[32,4,65]{2,1,0:T(4,128)(2,1)S(1)}, bf16[32,4,65]{2,1,0:T(4,128)(2,1)}, u32[]{:S(2)}) copy-start(bf16[32,4,65]{2,1,0:T(4,128)(2,1)} %param.13) | copy-start | bytes 49924
  112.6 3.4 copy-start.4
  175.0 27.5 %collective-permute-start.2 = (bf16[4,32,32,256]{3,2,0,1:T(8,128)(2,1)}, bf16[4,32,32,256]{3,2,0,1:T(8,128)(2,1)}, u32[]{:S(2)}, u32[]{:S(2)}) collective-permute-start(bf16[4,32,32,256]{3,2,0,1:T(8,128)(2,1)} %get-tuple-element.582), channel_id=1, source_target_pairs={{0,1},{1,2},{2,3},{3,4},{4,5},{5,6},{6,7},{7,8},{8,9},{9,10},{10,1... | collective-permute-start | bytes 6291464 | tf_op jit(solution)/shard_map/ppermute | solution.py:29
  196.6 16.2 %collective-permute-start.3 = (bf16[4,32,32,256]{3,2,0,1:T(8,128)(2,1)}, bf16[4,32,32,256]{3,2,0,1:T(8,128)(2,1)}, u32[]{:S(2)}, u32[]{:S(2)}) collective-permute-start(bf16[4,32,32,256]{3,2,0,1:T(8,128)(2,1)} %get-tuple-element.581), channel_id=1, source_target_pairs={{1,0},{2,1},{3,2},{4,3},{5,4},{6,5},{7,6},{8,7},{9,8},{10,9},{11,1... | collective-permute-start | bytes 6291464 | tf_op jit(solution)/shard_map/ppermute | solution.py:29
Sparse Core Ops, SparseCore 0:
  369.7 117.2 all-reduce.10
